TPU v7x, 256 devices: a whole 4x4x8 slice. The times are simulated.
256 devices in a mesh: dp: 32 (over y, z), fsdp: 8 (over x, core).
Axes of the slice: x: 4, y: 4, z: 8, core: 2. Of those that a mesh axis runs over, the one named last changes fastest.
Arguments:
- prefill_tokens: bfloat16 [16384, 2048], P('dp'), may hold values from -3 to 3
- decode_tokens: bfloat16 [128, 2048], P('dp'), may hold values from -3 to 3
- query_weight: bfloat16 [2048, 2048], P('dp', 'fsdp'), may hold values from -0.125 to 0.125
- key_weight: bfloat16 [2048, 2048], P('dp', 'fsdp'), may hold values from -0.125 to 0.125
- value_weight: bfloat16 [2048, 2048], P('dp', 'fsdp'), may hold values from -0.125 to 0.125
- out_weight: bfloat16 [2048, 2048], P('fsdp', 'dp'), may hold values from -0.125 to 0.125
- prior_keys: bfloat16 [32, 2048, 2048], P('dp', None, 'fsdp'), may hold values from -480 to 480
- prior_values: bfloat16 [32, 2048, 2048], P('dp', None, 'fsdp'), may hold values from -6 to 6
- prior_length: int32 [32], P('dp'), may hold values from 0 to 2048, as said below
- pool_keys: bfloat16 [1536, 128, 2048], P('dp', None, 'fsdp'), may hold values from -480 to 480
- pool_values: bfloat16 [1536, 128, 2048], P('dp', None, 'fsdp'), may hold values from -6 to 6
- page_slots: int32 [1536], replicated, may hold values from 0 to 1535, each once
- page_counts: int32 [128], replicated, may hold values from 1 to 128, 1536 in all
- last_fill: int32 [128], replicated, may hold values from 1 to 128
- decode_request: int32 [128], replicated, may hold values from 0 to 127, each once
Outputs:
- mixed_prefill: bfloat16 [16384, 2048], P('dp', 'fsdp')
- mixed_decode: bfloat16 [128, 2048], P('dp', 'fsdp')
Inputs may be any that keep to these rules, and one draw needn't show every extreme that they name: `prior_length`: one prefill request's prior fills all 2048 slots. Request r owns the logical pages first_page[r] to first_page[r] + page_counts[r] - 1; the counts sum to 1536, and some request has exactly 128 pages. A permutation: pool slot page_slots[k] holds logical page k. `decode_request`: A permutation of the decode requests.
All inputs are finite; a program needn't handle non-finite values.
Results may differ from a plain program's by a relative error of at most 0.015.
The roundings to bfloat16 on the way count: a program that leaves them out, or rounds other values in their place, can miss the bound.
Values may be sent and summed in bfloat16 or wider, within the bound.
No kernel may reach another device: no remote copies, remote signals or barrier semaphores. Data moves between devices by JAX's collectives and lax.ppermute only.
A program may use at most 128 MiB of HBM per device.

v0:
```python
import jax
import jax.numpy as jnp
from jax import lax
from jax.sharding import PartitionSpec as P

HEAD = 128
PAGE = 128
EPSILON = 1e-05
ROPE_BASE = 10000.0
NEG_FILL = -1e30


def merged(value, axis, join):
    pieces = jax.tree.map(lambda part: lax.all_gather(part, axis), value)
    head = jax.tree.map(lambda part: part[0], pieces)
    tail = jax.tree.map(lambda part: part[1:], pieces)
    total, _ = lax.scan(lambda total, share: (join(total, share), None), head, tail)
    return total


def layer_norm(rows_in):
    widened = rows_in.astype(jnp.float32)
    average = jnp.mean(widened, axis=-1, keepdims=True)
    centred = widened - average
    variance = jnp.mean(centred * centred, axis=-1, keepdims=True)
    return (centred * lax.rsqrt(variance + EPSILON)).astype(jnp.bfloat16)


def rotary(vectors, positions, head_size):
    row_count = vectors.shape[0]
    split_heads = vectors.reshape(row_count, -1, head_size)
    halfway = head_size // 2
    exponent = jnp.arange(halfway, dtype=jnp.float32) * (2.0 / head_size)
    frequency = jnp.power(jnp.float32(ROPE_BASE), -exponent)
    angles = positions.astype(jnp.float32)[:, None] * frequency[None, :]
    cosine = jnp.cos(angles)[:, None, :]
    sine_part = jnp.sin(angles)[:, None, :]
    leading = split_heads[..., :halfway]
    trailing = split_heads[..., halfway:]
    turned = jnp.concatenate(
        [leading * cosine - trailing * sine_part, trailing * cosine + leading * sine_part], axis=-1
    )
    return turned.reshape(row_count, -1)


def rescale(vectors, factor, head_size):
    shaped = vectors.reshape(vectors.shape[0], factor.shape[1], head_size)
    return (shaped * factor[:, :, None]).reshape(vectors.shape)


def combine_pair(earlier, later):
    early_top, early_total, early_mix = earlier
    late_top, late_total, late_mix = later
    joined_top = jnp.maximum(early_top, late_top)
    early_factor = jnp.exp(early_top - joined_top)
    late_factor = jnp.exp(late_top - joined_top)
    joined_total = early_total * early_factor + late_total * late_factor
    joined_mix = rescale(early_mix, early_factor, HEAD) + rescale(late_mix, late_factor, HEAD)
    return (joined_top, joined_total, joined_mix)


def per_device(
    prefill_tokens,
    decode_tokens,
    query_weight,
    key_weight,
    value_weight,
    out_weight,
    prior_keys,
    prior_values,
    prior_length,
    pool_keys,
    pool_values,
    page_slots,
    page_counts,
    last_fill,
    decode_request,
):
    group_rows = prefill_tokens.shape[0]
    decode_rows = decode_tokens.shape[0]
    local_width = query_weight.shape[1]
    head_count = local_width // HEAD
    score_scale = HEAD ** (-0.5)
    data_index = lax.axis_index("dp")
    model_index = lax.axis_index("fsdp")
    tokens = jnp.concatenate([prefill_tokens, decode_tokens], axis=0)
    normed = layer_norm(tokens)
    portions = (
        lax.all_gather(query_weight, "dp", axis=0, tiled=True),
        lax.all_gather(key_weight, "dp", axis=0, tiled=True),
        lax.all_gather(value_weight, "dp", axis=0, tiled=True),
    )
    raw_queries, raw_keys, raw_values = tuple(
        (jnp.dot(normed, portion, preferred_element_type=jnp.float32) for portion in portions)
    )
    cache_length = (page_counts - 1) * PAGE + last_fill
    first_page = jnp.cumsum(page_counts) - page_counts
    request_count = decode_request.shape[0]
    slot_numbers = jnp.arange(request_count, dtype=jnp.int32)
    slot_of_request = jnp.zeros((request_count,), jnp.int32).at[decode_request].set(slot_numbers)
    my_slots = data_index * decode_rows + jnp.arange(decode_rows, dtype=jnp.int32)
    my_requests = jnp.take(decode_request, my_slots)
    positions = jnp.concatenate(
        [
            prior_length[0] + jnp.arange(group_rows, dtype=jnp.int32),
            jnp.take(cache_length, my_requests),
        ]
    )
    queries = rotary(raw_queries, positions, HEAD).astype(jnp.bfloat16)
    keys_new = rotary(raw_keys, positions, HEAD).astype(jnp.bfloat16)
    values_new = raw_values.astype(jnp.bfloat16)
    prior_slots = prior_keys.shape[1]
    group_queries = queries[:group_rows].reshape(group_rows, head_count, HEAD)
    group_keys = keys_new[:group_rows].reshape(group_rows, head_count, HEAD)
    group_values = values_new[:group_rows].reshape(group_rows, head_count, HEAD)
    stored_keys = prior_keys[0].reshape(prior_slots, head_count, HEAD)
    stored_values = prior_values[0].reshape(prior_slots, head_count, HEAD)
    prior_scores = (
        jnp.einsum("qhd,khd->hqk", group_queries, stored_keys, preferred_element_type=jnp.float32)
        * score_scale
    )
    prior_live = jnp.arange(prior_slots, dtype=jnp.int32) < prior_length[0]
    prior_scores = jnp.where(prior_live[None, None, :], prior_scores, NEG_FILL)
    group_scores = (
        jnp.einsum("qhd,khd->hqk", group_queries, group_keys, preferred_element_type=jnp.float32)
        * score_scale
    )
    causal = jnp.arange(group_rows)[None, :] <= jnp.arange(group_rows)[:, None]
    group_scores = jnp.where(causal[None], group_scores, NEG_FILL)
    row_top = jnp.maximum(
        jnp.max(prior_scores, axis=2, keepdims=True), jnp.max(group_scores, axis=2, keepdims=True)
    )
    prior_weights = jnp.exp(prior_scores - row_top)
    group_weights = jnp.exp(group_scores - row_top)
    weight_total = jnp.sum(prior_weights, axis=2) + jnp.sum(group_weights, axis=2)
    combined = jnp.einsum(
        "hqk,khd->qhd",
        prior_weights.astype(jnp.bfloat16),
        stored_values,
        preferred_element_type=jnp.float32,
    )
    combined = combined + jnp.einsum(
        "hqk,khd->qhd",
        group_weights.astype(jnp.bfloat16),
        group_values,
        preferred_element_type=jnp.float32,
    )
    prefill_attended = (
        (combined / jnp.transpose(weight_total)[:, :, None])
        .reshape(group_rows, local_width)
        .astype(jnp.bfloat16)
    )
    own_queries = queries[group_rows:]
    slot_queries = lax.all_gather(own_queries, "dp", axis=0, tiled=True)
    pool_count = page_slots.shape[0]
    pool_local = pool_keys.shape[0]
    logical_of_slot = (
        jnp.zeros((pool_count,), jnp.int32)
        .at[page_slots]
        .set(jnp.arange(pool_count, dtype=jnp.int32))
    )
    local_logical = lax.dynamic_slice_in_dim(logical_of_slot, data_index * pool_local, pool_local)
    page_owner = (
        jnp.sum((first_page[None, :] <= local_logical[:, None]).astype(jnp.int32), axis=1) - 1
    )
    page_number = local_logical - jnp.take(first_page, page_owner)
    page_slot = jnp.take(slot_of_request, page_owner)
    page_queries = jnp.take(slot_queries, page_slot, axis=0).reshape(pool_local, head_count, HEAD)
    page_keys = pool_keys.reshape(pool_local, PAGE, head_count, HEAD)
    page_scores = (
        jnp.einsum("phd,pkhd->phk", page_queries, page_keys, preferred_element_type=jnp.float32)
        * score_scale
    )
    key_place = page_number[:, None] * PAGE + jnp.arange(PAGE, dtype=jnp.int32)[None, :]
    page_live = key_place < jnp.take(cache_length, page_owner)[:, None]
    page_scores = jnp.where(page_live[:, None, :], page_scores, NEG_FILL)
    member = page_slot[:, None] == slot_numbers[None, :]
    page_top = jnp.max(page_scores, axis=2)
    slot_top = jnp.max(jnp.where(member[:, :, None], page_top[:, None, :], NEG_FILL), axis=0)
    page_weights = jnp.exp(page_scores - jnp.take(slot_top, page_slot, axis=0)[:, :, None])
    member_weights = member.astype(jnp.float32)
    slot_total = jnp.dot(
        member_weights.T, jnp.sum(page_weights, axis=2), precision=lax.Precision.HIGHEST
    )
    page_values = pool_values.reshape(pool_local, PAGE, head_count, HEAD).astype(jnp.float32)
    page_mix = jnp.einsum(
        "phk,pkhd->phd", page_weights, page_values, precision=lax.Precision.HIGHEST
    )
    slot_mix = jnp.dot(
        member_weights.T, page_mix.reshape(pool_local, local_width), precision=lax.Precision.HIGHEST
    )
    merged_top, merged_total, merged_mix = merged(
        (slot_top, slot_total, slot_mix), "dp", combine_pair
    )
    mine_top = lax.dynamic_slice_in_dim(merged_top, data_index * decode_rows, decode_rows, 0)
    mine_total = lax.dynamic_slice_in_dim(merged_total, data_index * decode_rows, decode_rows, 0)
    mine_mix = lax.dynamic_slice_in_dim(merged_mix, data_index * decode_rows, decode_rows, 0)
    own_keys = keys_new[group_rows:].reshape(decode_rows, head_count, HEAD)
    own_score = (
        jnp.einsum(
            "rhd,rhd->rh",
            own_queries.reshape(decode_rows, head_count, HEAD),
            own_keys,
            preferred_element_type=jnp.float32,
        )
        * score_scale
    )
    final_top = jnp.maximum(mine_top, own_score)
    cache_factor = jnp.exp(mine_top - final_top)
    own_factor = jnp.exp(own_score - final_top)
    final_total = mine_total * cache_factor + own_factor
    final_mix = rescale(mine_mix, cache_factor, HEAD) + rescale(
        values_new[group_rows:].astype(jnp.float32), own_factor, HEAD
    )
    decode_attended = rescale(final_mix, 1.0 / final_total, HEAD).astype(jnp.bfloat16)
    attended = jnp.concatenate([prefill_attended, decode_attended], axis=0)
    residual = lax.dynamic_slice_in_dim(tokens, model_index * local_width, local_width, 1)
    terms = jnp.dot(
        attended,
        lax.all_gather(out_weight, "dp", axis=1, tiled=True),
        preferred_element_type=jnp.float32,
    )
    branch = lax.psum_scatter(
        terms.astype(jnp.bfloat16), "fsdp", scatter_dimension=1, tiled=True
    ).astype(jnp.float32)
    result = (residual.astype(jnp.float32) + branch).astype(jnp.bfloat16)
    return (result[:group_rows], result[group_rows:])


def solution(mesh):
    in_specs = (
        P("dp", None),
        P("dp", None),
        P("dp", "fsdp"),
        P("dp", "fsdp"),
        P("dp", "fsdp"),
        P("fsdp", "dp"),
        P("dp", None, "fsdp"),
        P("dp", None, "fsdp"),
        P("dp"),
        P("dp", None, "fsdp"),
        P("dp", None, "fsdp"),
        P(),
        P(),
        P(),
        P(),
    )
    out_specs = (P("dp", "fsdp"), P("dp", "fsdp"))
    return jax.shard_map(
        per_device, mesh=mesh, in_specs=in_specs, out_specs=out_specs, check_vma=False
    )
```

profile of v0, /device:TPU:8, one launch (start us, length us, event | category | flops | bytes accessed | tf_op | source)
XLA Modules:
  0.0 472.7 jit_solution(2688506723281561803)
XLA Ops:
  11.9 6.2 %scatter_custom_fusion.1 = s32[1536]{0:T(1024)S(1)} fusion(s32[1536]{0:T(1024)S(1)} %compare_select_fusion, s32[1536]{0:T(1024)S(1)} %iota.55, s32[]{:T(128)} %constant.45.clone.1), kind=kCustom, calls=%fused_computation.111 | custom fusion | bytes 6148 | tf_op jit(solution)/shard_map/scatter | solution.py:160
  24.2 4.7 %copy.120 = bf16[48,128,256]{1,2,0:T(8,128)(2,1)} copy(bf16[48,128,256]{2,1,0:T(8,128)(2,1)} %param.30) | data formatting | bytes 6291456 | tf_op jit(solution)/shard_map/reshape | solution.py:169
  28.9 1.7 constant_dynamic-update-slice_fusion.1
  31.8 1.9 fusion.9
  35.9 1.8 multiply_cosine_fusion
  37.9 50.8 %all-gather.10.cloned.1.call-done = bf16[2048,256]{1,0:T(8,128)(2,1)} async-done(((bf16[64,256]{1,0:T(8,128)(2,1)}), bf16[2048,256]{1,0:T(8,128)(2,1)}) %all-gather.10.cloned.1.call-update) | async-done | bytes 1048592 | tf_op jit(solution)/shard_map/all_gather | solution.py:89
  88.7 3.4 fusion.77
  92.1 2.1 reshape.284
  94.2 71.0 %all-gather.12.cloned.1.call-done = bf16[2048,256]{1,0:T(8,128)(2,1)} async-done(((bf16[64,256]{1,0:T(8,128)(2,1)}), bf16[2048,256]{1,0:T(8,128)(2,1)}) %all-gather.12.cloned.1.call-update) | async-done | bytes 1048592 | tf_op jit(solution)/shard_map/all_gather | solution.py:90
  165.2 3.4 fusion.78
  168.6 2.1 reshape.285
  170.7 2.7 fusion.74
  175.2 47.6 %all-gather.3 = bf16[32,4,256]{2,1,0:T(4,128)(2,1)S(1)} all-gather(bf16[1,4,256]{2,1,0:T(4,128)(2,1)S(1)} %bitcast.127), channel_id=1, replica_groups=mesh['dp'=32,'fsdp'=8] {'dp'}, dimensions={0}, use_global_device_ids=true | all-gather | bytes 67584 | tf_op jit(solution)/shard_map/all_gather | solution.py:154
  224.3 2.8 fusion.44
  230.5 2.5 fusion.13
  233.0 1.7 fusion.39
  236.2 2.3 copy.118
  238.4 2.2 reshape_squeeze.6
  240.6 41.6 %all-gather = f32[4096,2]{0,1:T(2,128)S(1)} all-gather(f32[128,2]{0,1:T(2,128)S(1)} %select_reduce_fusion), channel_id=2, replica_groups=mesh['dp'=32,'fsdp'=8] {'dp'}, dimensions={0}, use_global_device_ids=true | all-gather | bytes 33792 | tf_op jit(solution)/shard_map/all_gather | solution.py:14
  283.0 41.3 %all-gather.1 = f32[4096,2]{0,1:T(2,128)S(1)} all-gather(f32[128,2]{0,1:T(2,128)S(1)} %fusion.50), channel_id=3, replica_groups=mesh['dp'=32,'fsdp'=8] {'dp'}, dimensions={0}, use_global_device_ids=true | all-gather | bytes 33792 | tf_op jit(solution)/shard_map/all_gather | solution.py:14
  324.9 3.3 fusion.16
  328.3 1.6 fusion.3
  329.9 1.9 fusion.4
  331.8 2.8 fusion.19
  334.6 2.6 convolution_convert_fusion.1
  338.7 1.8 copy.119
  340.5 2.1 fusion.17
  342.6 3.2 fusion.24
  345.8 4.5 slice.113
  350.3 72.1 %while.14 = (s32[]{:T(128)}, f32[128,2]{0,1:T(2,128)S(1)}, f32[128,2]{0,1:T(2,128)S(1)}, f32[128,256]{1,0:T(8,128)S(1)}, f32[31,128,2]{1,2,0:T(2,128)}, /*index=...) while((s32[]{:T(128)}, f32[128,2]{0,1:T(2,128)S(1)}, f32[128,2]{0,1:T(2,128)S(1)}, ...), condition=%wide.region_14.17_spmd, body=%wide.region_13.16_spmd.sunk | while | flops 99842 | bytes 931941 | solution.py:17
  423.8 3.7 convolution_convert_fusion
  427.5 36.0 %reduce-scatter.2.cloned.1.call-done = bf16[516,256]{1,0:T(8,128)(2,1)} async-done(((bf16[516,2048]{1,0:T(8,128)(2,1)}), bf16[516,256]{1,0:T(8,128)(2,1)}) %reduce-scatter.2.cloned.1.call-update) | async-done | bytes 264208 | tf_op jit(solution)/shard_map/reduce_scatter | solution.py:223
  (316 shorter events, 99.7 us)
Async XLA Ops:
  7.2 223.3 %copy-start = (bf16[48,128,256]{2,1,0:T(8,128)(2,1)S(1)}, bf16[48,128,256]{2,1,0:T(8,128)(2,1)}, u32[]{:S(2)}) copy-start(bf16[48,128,256]{2,1,0:T(8,128)(2,1)} %param.31) | copy-start | bytes 9437188
  7.2 81.5 %all-gather.10.cloned.1.call-start = ((), (), s32[]{:S(2)}) async-start(), calls=%async_computation.1 | async-start | bytes 1081344 | tf_op jit(solution)/shard_map/all_gather | solution.py:89
  7.9 157.3 %all-gather.12.cloned.1.call-start = ((), (), s32[]{:S(2)}) async-start(), calls=%async_computation.2 | async-start | bytes 1081344 | tf_op jit(solution)/shard_map/all_gather | solution.py:90
  8.7 326.0 %all-gather.14.cloned.1.call-start = ((), (), s32[]{:S(2)}) async-start(), calls=%async_computation.3 | async-start | bytes 1081344 | tf_op jit(solution)/shard_map/all_gather | solution.py:91
  9.4 336.4 %all-gather.18.cloned.1.call-start = ((), (), s32[]{:S(2)}) async-start(), calls=%async_computation.6 | async-start | bytes 4325376 | tf_op jit(solution)/shard_map/all_gather | solution.py:14
  23.5 5.4 %copy-start.17 = (s32[48]{0:T(128)}, s32[48]{0:T(128)S(1)}, u32[]{:S(2)}) copy-start(s32[48]{0:T(128)S(1)} %get-tuple-element.103) | copy-start | bytes 580
  28.9 1.7 copy-start.15
  30.7 3.0 copy-start.1
  35.8 186.9 %copy-start.16 = (s32[1024]{0:T(1024)}, s32[1024]{0:T(1024)S(1)}, u32[]{:S(2)}) copy-start(s32[1024]{0:T(1024)S(1)} %pad_clamp_fusion) | copy-start | bytes 12292
  37.9 189.2 %copy-start.14 = (pred[48,128]{1,0:T(8,128)(4,1)}, pred[48,128]{1,0:T(8,128)(4,1)S(1)}, u32[]{:S(2)}) copy-start(pred[48,128]{1,0:T(8,128)(4,1)S(1)} %add_compare_fusion) | copy-start | bytes 18436
  170.7 2.7 copy-start.7
  170.7 2.7 copy-start.8
  173.7 0.7 copy-start.3
  173.7 1.4 copy-start.5
  173.7 1.4 copy-start.6
  233.0 49.8 %copy-start.18 = (s32[48]{0:T(128)S(1)}, s32[48]{0:T(128)}, u32[]{:S(2)}) copy-start(s32[48]{0:T(128)} %copy-done.17) | copy-start | bytes 580
  234.7 189.1 %all-gather.16.cloned.1.call-start = ((), (), s32[]{:S(2)}) async-start(), calls=%async_computation.4 | async-start | bytes 1081344 | tf_op jit(solution)/shard_map/all_gather | solution.py:220
  235.3 228.2 %reduce-scatter.2.cloned.1.call-start = ((), (), s32[]{:S(2)}) async-start(), calls=%async_computation.5 | async-start | bytes 2396160 | tf_op jit(solution)/shard_map/reduce_scatter | solution.py:223
  240.6 87.7 %copy-start.2 = (bf16[2048,2,128]{2,1,0:T(2,128)(2,1)S(1)}, bf16[2048,2,128]{2,1,0:T(2,128)(2,1)}, u32[]{:S(2)}) copy-start(bf16[2048,2,128]{2,1,0:T(2,128)(2,1)} %reshape_squeeze.6) | copy-start | bytes 3145732
  240.6 87.7 %copy-start.4 = (bf16[516,2,64]{2,0,1:T(8,128)(2,1)S(1)}, bf16[516,2,64]{2,0,1:T(8,128)(2,1)}, u32[]{:S(2)}) copy-start(bf16[516,2,64]{2,0,1:T(8,128)(2,1)} %copy-done.3) | copy-start | bytes 396292
  282.2 47.7 %copy-start.12 = (f32[4096,2]{0,1:T(2,128)}, f32[4096,2]{0,1:T(2,128)S(1)}, u32[]{:S(2)}) copy-start(f32[4096,2]{0,1:T(2,128)S(1)} %all-gather) | copy-start | bytes 98308
  324.3 5.6 %copy-start.13 = (f32[4096,2]{0,1:T(2,128)}, f32[4096,2]{0,1:T(2,128)S(1)}, u32[]{:S(2)}) copy-start(f32[4096,2]{0,1:T(2,128)S(1)} %all-gather.1) | copy-start | bytes 98308
  329.9 1.9 copy-start.10
  334.6 5.9 %copy-start.9 = (pred[512,512]{0,1:T(8,128)(4,1)S(1)}, pred[512,512]{0,1:T(8,128)(4,1)}, u32[]{:S(2)}) copy-start(pred[512,512]{0,1:T(8,128)(4,1)} %iota_compare_fusion) | copy-start | bytes 786436
  337.3 0.7 copy-start.11
  345.8 4.5 slice-start
  345.8 4.5 slice-start.1
  345.8 4.5 slice-start.2
  350.3 72.1 %copy-start.19 = (f32[4,2]{0,1:T(2,128)S(1)}, f32[4,2]{0,1:T(2,128)}, u32[]{:S(2)}) copy-start(f32[4,2]{0,1:T(2,128)} %get-tuple-element.104) | copy-start | bytes 100
Sparse Core Ops, SparseCore 0:
  10.6 78.0 all-gather.9
  91.3 73.8 all-gather.11
  167.8 73.8 all-gather.13
  244.1 79.1 all-gather.17
  325.7 73.2 all-gather.15
  427.6 35.8 reduce-scatter.1
where the time goes:
time: 475 us; the launch traced here: 473 us
  waiting for transfers between devices  160 us (34%)
  blocking collectives  130 us (27%)
  other arithmetic  72 us (15%)
  local copies, waits for them, and re-layouts  62.6 us (13%)
  matrix products  31.2 us (7%)
  between operations  15.1 us (3%)
    all_gather x2, blocking collectives, merged(): pieces = jax.tree.map(lambda part: lax.all_gather(part, axis), value)  82.9 us
    all_gather x1, waiting for transfers between devices, per_device(): lax.all_gather(key_weight, 'dp', axis=0, tiled=True)  71 us
    all_gather x1, waiting for transfers between devices, per_device(): lax.all_gather(query_weight, 'dp', axis=0, tiled=True)  50.8 us
    all_gather x1, blocking collectives, per_device(): slot_queries = lax.all_gather(own_queries, 'dp', axis=0, tiled=True)  47.6 us
    reduce_scatter x1, waiting for transfers between devices, per_device(): lax.psum_scatter(terms.astype(jnp.bfloat16), 'fsdp', scatter_dimension=1,...  36 us
    add x31, other arithmetic, combine_pair(): rescale(early_mix, early_factor, HEAD)  30.6 us
    add x31, other arithmetic, combine_pair(): joined_total = early_total * early_factor + late_total * late_factor  21.6 us
    mul x62, local copies, waits for them, and re-layouts, rescale(): return (shaped * factor[:, :, None]).reshape(vectors.shape)  12.2 us
  transfers between devices with their start and end apart: 6, of which 3 were waited for; matrix products, arithmetic and copies ran while one was open for 34% of the time, Pallas kernels for 0%

commit v1 on v0

--- a/solution.py
+++ b/solution.py
@@ -151,7 +151,10 @@
         .astype(jnp.bfloat16)
     )
     own_queries = queries[group_rows:]
-    slot_queries = lax.all_gather(own_queries, "dp", axis=0, tiled=True)
+    find_pages = lambda xs: jnp.concatenate(
+        jax.lax.all_to_all(jnp.stack([xs for _ in range(jax.lax.axis_size("dp"))]), "dp", 0, 0), 0
+    )
+    slot_queries = find_pages(own_queries)
     pool_count = page_slots.shape[0]
     pool_local = pool_keys.shape[0]
     logical_of_slot = (

time: 475 us -> 449 us (0.945)
  blocking collectives: 130 us -> 83.1 us
  waiting for transfers between devices: 160 us -> 199 us
  other arithmetic: 72 us -> 49 us
  starting transfers between devices: 0.23 us -> 7.91 us
    all_gather x1 -> x0, blocking collectives: 47.6 us -> none  [per_device(): slot_queries = lax.all_gather(own_queries, 'dp', axis=0, tiled=True)]
    all_gather x1, waiting for transfers between devices: 0.01 us -> 22 us  [per_device(): lax.all_gather(value_weight, 'dp', axis=0, tiled=True)]
    add x31, other arithmetic: 21.6 us -> 0.78 us  [combine_pair(): joined_total = early_total * early_factor + late_total * late_factor]
    all_gather x1, waiting for transfers between devices: 50.8 us -> 58.9 us  [per_device(): lax.all_gather(query_weight, 'dp', axis=0, tiled=True)]
    all_to_all x0 -> x1, starting transfers between devices: none -> 7.49 us  [per_device(): jax.lax.all_to_all(jnp.stack([xs for _ in range(jax.lax.axis_size('dp'))]...]
    all_gather x1, waiting for transfers between devices: 0.01 us -> 5.8 us  [per_device(): lax.all_gather(out_weight, 'dp', axis=1, tiled=True)]
  transfers between devices with their start and end apart: 6 -> 7, of which waited for: 3 -> 6; matrix products, arithmetic and copies ran while one was open for 34% -> 30% of each run, Pallas kernels for 0% -> 0%
where the time goes in v1:
time: 449 us; the launch traced here: 447 us
  waiting for transfers between devices  199 us (44%)
  blocking collectives  83.1 us (19%)
  local copies, waits for them, and re-layouts  60.7 us (14%)
  other arithmetic  49 us (11%)
  matrix products  31.3 us (7%)
  between operations  15.2 us (3%)
  starting transfers between devices  7.91 us (2%)
    all_gather x2, blocking collectives, merged(): pieces = jax.tree.map(lambda part: lax.all_gather(part, axis), value)  83.1 us
    all_gather x1, waiting for transfers between devices, per_device(): lax.all_gather(key_weight, 'dp', axis=0, tiled=True)  70.9 us
    all_gather x1, waiting for transfers between devices, per_device(): lax.all_gather(query_weight, 'dp', axis=0, tiled=True)  58.9 us
    reduce_scatter x1, waiting for transfers between devices, per_device(): lax.psum_scatter(terms.astype(jnp.bfloat16), 'fsdp', scatter_dimension=1,...  35.3 us
    add x31, other arithmetic, combine_pair(): rescale(early_mix, early_factor, HEAD)  30.6 us
    all_gather x1, waiting for transfers between devices, per_device(): lax.all_gather(value_weight, 'dp', axis=0, tiled=True)  22 us
    mul x62, local copies, waits for them, and re-layouts, rescale(): return (shaped * factor[:, :, None]).reshape(vectors.shape)  12.3 us
    dot_general x3, matrix products, per_device(): jnp.dot(normed, portion, preferred_element_type=jnp.float32)  9.45 us
  transfers between devices with their start and end apart: 7, of which 6 were waited for; matrix products, arithmetic and copies ran while one was open for 30% of the time, Pallas kernels for 0%

profile of v1, /device:TPU:8, one launch (start us, length us, event | category | flops | bytes accessed | tf_op | source)
XLA Modules:
  0.0 447.3 jit_solution(3134942566266047627)
XLA Ops:
  12.4 1.9 fusion.9
  14.7 6.2 %scatter_custom_fusion.1 = s32[1536]{0:T(1024)S(1)} fusion(s32[1536]{0:T(1024)S(1)} %compare_select_fusion, s32[1536]{0:T(1024)S(1)} %iota.55, s32[]{:T(128)} %constant.45.clone.1), kind=kCustom, calls=%fused_computation.111 | custom fusion | bytes 6148 | tf_op jit(solution)/shard_map/scatter | solution.py:163
  27.8 1.9 multiply_cosine_fusion
  29.8 58.9 %all-gather.9.cloned.1.call-done = bf16[2048,256]{1,0:T(8,128)(2,1)} async-done(((bf16[64,256]{1,0:T(8,128)(2,1)}), bf16[2048,256]{1,0:T(8,128)(2,1)}) %all-gather.9.cloned.1.call-update) | async-done | bytes 1048592 | tf_op jit(solution)/shard_map/all_gather | solution.py:89
  88.7 3.4 fusion.77
  92.1 2.1 reshape.289
  94.2 70.9 %all-gather.11.cloned.1.call-done = bf16[2048,256]{1,0:T(8,128)(2,1)} async-done(((bf16[64,256]{1,0:T(8,128)(2,1)}), bf16[2048,256]{1,0:T(8,128)(2,1)}) %all-gather.11.cloned.1.call-update) | async-done | bytes 1048592 | tf_op jit(solution)/shard_map/all_gather | solution.py:90
  165.2 3.4 fusion.78
  168.6 2.1 reshape.290
  170.7 2.7 fusion.74
  175.9 7.5 %all-to-all-start = ((bf16[32,4,256]{2,1,0:T(4,128)(2,1)}), bf16[32,4,256]{2,1,0:T(4,128)(2,1)S(1)}, u32[]{:S(2)}, u32[]{:S(2)}) async-start(bf16[32,4,256]{2,1,0:T(4,128)(2,1)} %stack.2), calls=%async_computation | async-start | bytes 131072 | tf_op jit(solution)/shard_map/all_to_all | solution.py:155
  183.6 4.7 %copy.102 = bf16[48,128,256]{1,2,0:T(8,128)(2,1)} copy(bf16[48,128,256]{2,1,0:T(8,128)(2,1)} %param.30) | data formatting | bytes 6291456 | tf_op jit(solution)/shard_map/reshape | solution.py:172
  188.4 3.8 all-to-all-done
  193.6 2.8 fusion.44
  199.8 2.5 fusion.13
  205.4 2.3 copy.100
  207.7 2.1 reshape_squeeze.6
  209.8 3.5 fusion.16
  214.9 1.9 fusion.4
  216.8 2.9 fusion.19
  219.7 22.0 %all-gather.13.cloned.1.call-done = bf16[2048,256]{1,0:T(8,128)(2,1)} async-done(((bf16[64,256]{1,0:T(8,128)(2,1)}), bf16[2048,256]{1,0:T(8,128)(2,1)}) %all-gather.13.cloned.1.call-update) | async-done | bytes 1048592 | tf_op jit(solution)/shard_map/all_gather | solution.py:91
  241.7 2.6 convolution_convert_fusion.1
  245.7 1.8 copy.101
  247.5 2.1 fusion.17
  249.6 3.2 fusion.24
  252.8 41.4 %all-gather = f32[4096,2]{0,1:T(2,128)S(1)} all-gather(f32[128,2]{0,1:T(2,128)S(1)} %select_reduce_fusion), channel_id=2, replica_groups=mesh['dp'=32,'fsdp'=8] {'dp'}, dimensions={0}, use_global_device_ids=true | all-gather | bytes 33792 | tf_op jit(solution)/shard_map/all_gather | solution.py:14
  294.4 41.7 %all-gather.1 = f32[4096,2]{0,1:T(2,128)S(1)} all-gather(f32[128,2]{0,1:T(2,128)S(1)} %fusion.50), channel_id=3, replica_groups=mesh['dp'=32,'fsdp'=8] {'dp'}, dimensions={0}, use_global_device_ids=true | all-gather | bytes 33792 | tf_op jit(solution)/shard_map/all_gather | solution.py:14
  336.2 4.5 %slice.113 = f32[3968,256]{1,0:T(8,128)} slice(f32[4096,256]{1,0:T(8,128)} %all-gather.17.cloned.1.call-done), slice={[128:4096], [0:256]} | slice | bytes 8126464 | tf_op jit(solution)/shard_map/slice | solution.py:16
  340.6 51.3 %while.14 = (s32[]{:T(128)}, f32[128,2]{0,1:T(2,128)S(1)}, f32[128,2]{0,1:T(2,128)S(1)}, f32[128,256]{1,0:T(8,128)S(1)}, f32[31,128,2]{1,2,0:T(2,128)S(1)}, /*in...) while((s32[]{:T(128)}, f32[128,2]{0,1:T(2,128)S(1)}, f32[128,2]{0,1:T(2,128)S(1)}, ...), condition=%wide.region_14.17_spmd, body=%wide.region_13.16_spmd.sunk | while | flops 99842 | bytes 931941 | solution.py:17
  393.3 5.8 %all-gather.15.cloned.1.call-done = bf16[256,2048]{0,1:T(8,128)(2,1)} async-done(((bf16[256,64]{0,1:T(8,128)(2,1)}), bf16[256,2048]{0,1:T(8,128)(2,1)}) %all-gather.15.cloned.1.call-update) | async-done | bytes 1048592 | tf_op jit(solution)/shard_map/all_gather | solution.py:223
  399.1 3.6 convolution_convert_fusion
  402.8 35.3 %reduce-scatter.2.cloned.1.call-done = bf16[516,256]{1,0:T(8,128)(2,1)} async-done(((bf16[516,2048]{1,0:T(8,128)(2,1)}), bf16[516,256]{1,0:T(8,128)(2,1)}) %reduce-scatter.2.cloned.1.call-update) | async-done | bytes 264208 | tf_op jit(solution)/shard_map/reduce_scatter | solution.py:226
  (320 shorter events, 79.9 us)
Async XLA Ops:
  7.2 192.6 %copy-start = (bf16[48,128,256]{2,1,0:T(8,128)(2,1)S(1)}, bf16[48,128,256]{2,1,0:T(8,128)(2,1)}, u32[]{:S(2)}) copy-start(bf16[48,128,256]{2,1,0:T(8,128)(2,1)} %param.31) | copy-start | bytes 9437188
  7.2 4.0 copy-start.14
  7.2 81.5 %all-gather.9.cloned.1.call-start = ((), (), s32[]{:S(2)}) async-start(), calls=%async_computation.2 | async-start | bytes 1081344 | tf_op jit(solution)/shard_map/all_gather | solution.py:89
  7.9 157.3 %all-gather.11.cloned.1.call-start = ((), (), s32[]{:S(2)}) async-start(), calls=%async_computation.3 | async-start | bytes 1081344 | tf_op jit(solution)/shard_map/all_gather | solution.py:90
  8.7 233.0 %all-gather.13.cloned.1.call-start = ((), (), s32[]{:S(2)}) async-start(), calls=%async_computation.4 | async-start | bytes 1081344 | tf_op jit(solution)/shard_map/all_gather | solution.py:91
  11.2 3.1 copy-start.2
  11.6 2.7 copy-start.20
  11.6 3.1 copy-start.15
  11.6 3.1 copy-start.21
  11.6 9.6 %copy-start.1 = (s32[128]{0:T(128)S(1)}, s32[128]{0:T(128)}, u32[]{:S(2)}) copy-start(s32[128]{0:T(128)} %param.35) | copy-start | bytes 1540
  27.1 156.5 %copy-start.17 = (s32[48]{0:T(128)}, s32[48]{0:T(128)S(1)}, u32[]{:S(2)}) copy-start(s32[48]{0:T(128)S(1)} %get-tuple-element.96) | copy-start | bytes 580
  29.8 166.7 %copy-start.13 = (pred[48,128]{1,0:T(8,128)(4,1)}, pred[48,128]{1,0:T(8,128)(4,1)S(1)}, u32[]{:S(2)}) copy-start(pred[48,128]{1,0:T(8,128)(4,1)S(1)} %add_compare_fusion) | copy-start | bytes 18436
  170.7 2.7 copy-start.8
  170.7 2.7 copy-start.9
  173.8 0.7 copy-start.4
  173.8 1.4 copy-start.6
  173.8 1.4 copy-start.7
  175.9 16.3 %all-to-all-start = ((bf16[32,4,256]{2,1,0:T(4,128)(2,1)}), bf16[32,4,256]{2,1,0:T(4,128)(2,1)S(1)}, u32[]{:S(2)}, u32[]{:S(2)}) async-start(bf16[32,4,256]{2,1,0:T(4,128)(2,1)} %stack.2), calls=%async_computation | async-start | bytes 131072 | tf_op jit(solution)/shard_map/all_to_all | solution.py:155
  183.4 152.8 %all-gather.17.cloned.1.call-start = ((), (), s32[]{:S(2)}) async-start(), calls=%async_computation.7 | async-start | bytes 4325376 | tf_op jit(solution)/shard_map/all_gather | solution.py:14
  188.4 8.1 %copy-start.16 = (s32[1024]{0:T(1024)}, s32[1024]{0:T(1024)S(1)}, u32[]{:S(2)}) copy-start(s32[1024]{0:T(1024)S(1)} %pad_clamp_fusion) | copy-start | bytes 12292
  204.0 195.1 %all-gather.15.cloned.1.call-start = ((), (), s32[]{:S(2)}) async-start(), calls=%async_computation.5 | async-start | bytes 1081344 | tf_op jit(solution)/shard_map/all_gather | solution.py:223
  204.6 233.5 %reduce-scatter.2.cloned.1.call-start = ((), (), s32[]{:S(2)}) async-start(), calls=%async_computation.6 | async-start | bytes 2396160 | tf_op jit(solution)/shard_map/reduce_scatter | solution.py:226
  209.8 3.5 copy-start.3
  209.8 3.5 copy-start.5
  214.9 1.9 copy-start.11
  219.6 27.8 %copy-start.10 = (pred[512,512]{0,1:T(8,128)(4,1)S(1)}, pred[512,512]{0,1:T(8,128)(4,1)}, u32[]{:S(2)}) copy-start(pred[512,512]{0,1:T(8,128)(4,1)} %iota_compare_fusion) | copy-start | bytes 786436
  244.3 0.7 copy-start.12
  249.6 44.6 %copy-start.18 = (s32[48]{0:T(128)S(1)}, s32[48]{0:T(128)}, u32[]{:S(2)}) copy-start(s32[48]{0:T(128)} %copy-done.17) | copy-start | bytes 580
  336.2 4.5 %slice-start = ((f32[4096,256]{1,0:T(8,128)}), f32[128,256]{1,0:T(8,128)S(1)}, s32[]{:S(2)}) async-start(f32[4096,256]{1,0:T(8,128)} %all-gather.17.cloned.1.call-done), calls=%async_computation.8 | async-start | bytes 262144 | tf_op jit(solution)/shard_map/slice | solution.py:15
  340.6 51.3 %copy-start.19 = (f32[4,2]{0,1:T(2,128)S(1)}, f32[4,2]{0,1:T(2,128)}, u32[]{:S(2)}) copy-start(f32[4,2]{0,1:T(2,128)} %get-tuple-element.97) | copy-start | bytes 100
Sparse Core Ops, SparseCore 0:
  10.6 78.0 all-gather.8
  91.3 73.8 all-gather.10
  167.8 73.8 all-gather.12
  244.1 79.1 all-gather.16
  325.7 73.3 all-gather.14
  402.9 35.1 reduce-scatter.1
